TPU v7x, 256 devices: a whole 4x4x8 slice. The times are simulated.
256 devices in a mesh: tok: 32 (over z, x), tp: 8 (over y, core).
Axes of the slice: x: 4, y: 4, z: 8, core: 2. Of those that a mesh axis runs over, the one named last changes fastest.
Arguments:
- tokens: bfloat16 [16384, 8192], P('tok', 'tp'), may hold values from -6 to 6
- frozen_weight: bfloat16 [8192, 2048], P('tp'), may hold values from -0.0625 to 0.0625
- adapter_down_matrices: bfloat16 [256, 8192, 64], P('tok', 'tp'), may hold values from -0.0625 to 0.0625
- adapter_up_matrices: bfloat16 [256, 64, 2048], P('tok', None, 'tp'), may hold values from -0.75 to 0.75
- adapter_per_block: int32 [1024], P('tok'), may hold values from 0 to 255, as said below
- slot_per_adapter: int32 [256], replicated, may hold values from 0 to 255, as said below
- rank_per_adapter: int32 [256], replicated, may hold values from 16 to 64
- output_gradient: bfloat16 [16384, 2048], P('tok', 'tp'), may hold values from -6 to 6
Outputs:
- projected: bfloat16 [16384, 2048], P('tok', 'tp')
- token_gradient: bfloat16 [16384, 8192], P('tok', 'tp')
- grad_down: float32 [256, 8192, 64], P('tok', 'tp')
- grad_up: float32 [256, 64, 2048], P('tok', None, 'tp')
Inputs may be any that keep to these rules, and one draw needn't show every extreme that they name: `adapter_per_block`: block b covers tokens b * 16 to (b + 1) * 16 - 1. Among the blocks of one index of tok, at most 2 have adapters stored on any one index of tok (slots k with k // 8 equal), and one index of tok receives exactly 2 such blocks from every index. A permutation: adapter a is stored in slot slot_per_adapter[a] of adapter_down_matrices and adapter_up_matrices.
All inputs are finite; a program needn't handle non-finite values.
Results may differ from a plain program's by a relative error of at most 0.0033.
Values may be sent and summed in bfloat16 or wider, within the bound.
No kernel may reach another device: no remote copies, remote signals or barrier semaphores. Data moves between devices by JAX's collectives and lax.ppermute only.
A program may use at most 128 MiB of HBM per device.

v0:
```python
import jax
import jax.numpy as jnp
from jax import lax
from jax.sharding import PartitionSpec as P

ALPHA = 32
BLOCK_TOKENS = 16


def route(block_slot, number_adapters, capacity):
    owner_ids = block_slot // number_adapters
    block_ids = jnp.arange(block_slot.shape[-1], dtype=jnp.int32)
    earlier = (owner_ids[..., :, None] == owner_ids[..., None, :]) & (
        block_ids[None, :] < block_ids[:, None]
    )
    position = jnp.sum(earlier.astype(jnp.int32), axis=-1)
    return owner_ids * capacity + position


def per_device(
    tokens,
    frozen_weight,
    adapter_down_matrices,
    adapter_up_matrices,
    adapter_per_block,
    slot_per_adapter,
    rank_per_adapter,
    output_gradient,
):
    tok_count = lax.axis_size("tok")
    me = lax.axis_index("tok")
    token_rows, width_portion = tokens.shape
    column_portion = output_gradient.shape[1]
    block_count = adapter_per_block.shape[0]
    number_adapters, _, rank_ceiling = adapter_down_matrices.shape
    capacity = max(2, 2 * block_count // tok_count)
    slots = tok_count * capacity
    row_total = slots * BLOCK_TOKENS
    lane = width_portion + column_portion
    block_slot = jnp.take(slot_per_adapter, adapter_per_block)
    destination = route(block_slot, number_adapters, capacity)
    slot_ids = jnp.arange(slots, dtype=jnp.int32)
    hit = destination[None, :] == slot_ids[:, None]
    filled = jnp.any(hit, axis=1)
    source_block = jnp.sum(
        jnp.where(hit, jnp.arange(block_count, dtype=jnp.int32)[None, :], 0), axis=1
    )
    packed = jnp.concatenate(
        [
            tokens.reshape(block_count, BLOCK_TOKENS, width_portion),
            output_gradient.reshape(block_count, BLOCK_TOKENS, column_portion),
        ],
        axis=2,
    )
    send = jnp.where(filled[:, None, None], jnp.take(packed, source_block, axis=0), 0)
    arrived = lax.all_to_all(send, "tok", split_axis=0, concat_axis=0, tiled=True)
    all_blocks = lax.all_gather(adapter_per_block, "tok", axis=0, tiled=False)
    all_slot = jnp.take(slot_per_adapter, all_blocks)
    all_dest = route(all_slot, number_adapters, capacity)
    here = (
        all_dest[:, :, None]
        == (me * capacity + jnp.arange(capacity, dtype=jnp.int32))[None, None, :]
    )
    slot_local = jnp.where(here, (all_slot % number_adapters)[:, :, None] + 1, 0).sum(axis=1) - 1
    slot_adapter = slot_local.reshape(slots)
    input_rows = arrived[:, :, :width_portion].reshape(row_total, width_portion)
    grad_rows = arrived[:, :, width_portion:].reshape(row_total, column_portion)
    stored_ids = me * number_adapters + jnp.arange(number_adapters, dtype=jnp.int32)
    stored_match = slot_per_adapter[None, :] == stored_ids[:, None]
    stored_rank = jnp.sum(jnp.where(stored_match, rank_per_adapter[None, :], 0), axis=1)
    stored_scale = jnp.where(
        stored_rank > 0, jnp.float32(ALPHA) / jnp.maximum(stored_rank, 1).astype(jnp.float32), 0.0
    )
    chosen = slot_adapter[:, None] == jnp.arange(number_adapters, dtype=jnp.int32)[None, :]
    chosen_rows = jnp.broadcast_to(
        chosen[:, None, :], (slots, BLOCK_TOKENS, number_adapters)
    ).reshape(row_total, number_adapters)
    chosen_float = chosen_rows.astype(jnp.float32)
    row_rank = jnp.sum(jnp.where(chosen_rows, stored_rank[None, :], 0), axis=1)
    scale_per_row = jnp.sum(chosen_float * stored_scale[None, :], axis=1)
    keep_cols = jnp.arange(rank_ceiling, dtype=jnp.int32)[None, :] < row_rank[:, None]
    reduced_every_row = jnp.einsum(
        "ue,meb->umb", input_rows, adapter_down_matrices, preferred_element_type=jnp.float32
    )
    low_part = jnp.sum(reduced_every_row * chosen_float[:, :, None], axis=1)
    gathered_every_row = jnp.einsum(
        "hs,gbs->hgb", grad_rows, adapter_up_matrices, preferred_element_type=jnp.float32
    )
    pull_part = jnp.sum(gathered_every_row * chosen_float[:, :, None], axis=1)
    both = lax.psum(jnp.concatenate([low_part, pull_part], axis=1), "tp")
    low_sum = both[:, :rank_ceiling]
    pull_sum = both[:, rank_ceiling:]
    reduced_rows = jnp.where(keep_cols, low_sum, 0.0).astype(jnp.bfloat16)
    reduced_gradient = (scale_per_row[:, None] * jnp.where(keep_cols, pull_sum, 0.0)).astype(
        jnp.bfloat16
    )
    chosen_half = chosen_rows.astype(jnp.bfloat16)
    reduced_picked = chosen_half[:, :, None] * reduced_rows[:, None, :]
    gradient_picked = chosen_half[:, :, None] * reduced_gradient[:, None, :]
    adapter_increment = scale_per_row[:, None] * jnp.einsum(
        "hnq,nqs->hs", reduced_picked, adapter_up_matrices, preferred_element_type=jnp.float32
    )
    grad_down = jnp.einsum(
        "rd,rak->adk", input_rows, gradient_picked, preferred_element_type=jnp.float32
    )
    grad_up = stored_scale[:, None, None] * jnp.einsum(
        "rak,rc->akc", reduced_picked, grad_rows, preferred_element_type=jnp.float32
    )
    adapter_output_rows = jnp.einsum(
        "ymf,mcf->yc", gradient_picked, adapter_down_matrices, preferred_element_type=jnp.float32
    )
    back = jnp.concatenate(
        [
            adapter_output_rows.reshape(slots, BLOCK_TOKENS, width_portion),
            adapter_increment.reshape(slots, BLOCK_TOKENS, column_portion),
        ],
        axis=2,
    )
    returned = lax.all_to_all(back, "tok", split_axis=0, concat_axis=0, tiled=True)
    mine = jnp.take(returned, destination, axis=0)
    base_out = lax.psum_scatter(
        lax.dot_general(
            frozen_weight, tokens, (((0,), (1,)), ((), ())), preferred_element_type=jnp.float32
        ),
        "tp",
        scatter_dimension=0,
        tiled=True,
    ).T
    frozen_input_gradient = lax.dot_general(
        lax.all_gather(output_gradient, "tp", axis=1, tiled=True),
        frozen_weight,
        (((1,), (1,)), ((), ())),
        preferred_element_type=jnp.float32,
    )
    projected = (base_out + mine[:, :, width_portion:].reshape(token_rows, column_portion)).astype(
        jnp.bfloat16
    )
    token_gradient = (
        frozen_input_gradient + mine[:, :, :width_portion].reshape(token_rows, width_portion)
    ).astype(jnp.bfloat16)
    return (projected, token_gradient, grad_down, grad_up)


def solution(mesh):
    return jax.shard_map(
        per_device,
        mesh=mesh,
        in_specs=(
            P("tok", "tp"),
            P("tp", None),
            P("tok", "tp", None),
            P("tok", None, "tp"),
            P("tok"),
            P(),
            P(),
            P("tok", "tp"),
        ),
        out_specs=(P("tok", "tp"), P("tok", "tp"), P("tok", "tp", None), P("tok", None, "tp")),
        check_vma=False,
    )
```

profile of v0, /device:TPU:27, one launch (start us, length us, event | category | flops | bytes accessed | tf_op | source)
XLA Modules:
  0.0 338.1 jit_solution(13137650032125103438)
XLA Ops:
  7.9 1.4 gather_fusion
  10.4 1.4 pad_maximum_fusion.1
  11.8 2.2 gather_fusion.2
  14.1 3.7 %select_select_fusion = bf16[64,16,1280]{2,1,0:T(8,128)(2,1)} fusion(bf16[64,16,1280]{2,1,0:T(8,128)(2,1)} %gather_fusion.2, pred[64]{0:T(512)(128)(4,1)S(1)} %compare_and_fusion, pred[64]{0:T(512)(128)(4,1)S(1)} %fusion.30), kind=kLoop, calls=%fused_computation.5 | loop fusion | flops 2621440 | bytes 5243008 | tf_op jit(solution)/shard_map/jit(_where)/select_n | solution.py:55
  17.7 11.2 %all-to-all-start = ((bf16[64,16,1280]{2,1,0:T(8,128)(2,1)}), bf16[64,16,1280]{2,1,0:T(8,128)(2,1)}, u32[]{:S(2)}, u32[]{:S(2)}) async-start(bf16[64,16,1280]{2,1,0:T(8,128)(2,1)} %select_select_fusion), calls=%async_computation.1 | async-start | bytes 5242880 | tf_op jit(solution)/shard_map/all_to_all | solution.py:56
  30.5 61.4 %all-reduce = s32[1024]{0:T(1024)S(1)} all-reduce(s32[1024]{0:T(1024)S(1)} %dynamic-update-slice), channel_id=2, replica_groups=mesh['tok'=32,'tp'=8] {'tok'}, use_global_device_ids=true, to_apply=%add | all-reduce | flops 1024 | bytes 8192
  92.1 6.8 %gather_fusion.1 = s32[1024]{0:T(1024)S(1)} fusion(s32[256]{0:T(256)S(1)} %copy-done.1, s32[1024]{0:T(1024)S(1)} %broadcast_clamp_fusion), kind=kCustom, calls=%fused_computation.1 | custom fusion | bytes 12288 | tf_op jit(solution)/shard_map/jit(_take)/gather | solution.py:58
  100.6 1.8 slice.32
  102.5 1.3 fusion.37
  104.0 1.1 slice.33
  107.3 7.0 %fusion.36 = f32[2048,512]{1,0:T(8,128)} fusion(bf16[1024,2048]{1,0:T(8,128)(2,1)} %param.9, bf16[512,1024]{1,0:T(8,128)(2,1)} %param.8), kind=kOutput, calls=%fused_computation.86 | convolution fusion | flops 2147483648 | bytes 9437184 | tf_op jit(solution)/shard_map/dot_general | solution.py:122
  116.0 57.9 %all-reduce.3.cloned.1.call-done = f32[1024,128]{0,1:T(8,128)} async-done(((f32[1024,128]{0,1:T(8,128)}), f32[1024,128]{0,1:T(8,128)}) %all-reduce.3.cloned.1.call-update) | async-done | bytes 524304 | tf_op jit(solution)/shard_map/psum | solution.py:90
  174.9 1.5 fusion.11
  176.4 1.3 fusion.6
  177.7 2.9 pad_maximum_fusion
  180.6 9.6 %all-to-all-start.1 = ((f32[64,16,1280]{2,1,0:T(8,128)}), f32[64,16,1280]{2,1,0:T(8,128)}, u32[]{:S(2)}, u32[]{:S(2)}) async-start(f32[64,16,1280]{2,1,0:T(8,128)} %pad_maximum_fusion), calls=%async_computation.2 | async-start | bytes 10485760 | tf_op jit(solution)/shard_map/all_to_all | solution.py:119
  191.0 2.3 fusion.14
  193.3 2.6 convolution_bitcast_fusion
  195.9 116.9 %all-to-all-done.1 = f32[64,16,1280]{2,1,0:T(8,128)} async-done(((f32[64,16,1280]{2,1,0:T(8,128)}), f32[64,16,1280]{2,1,0:T(8,128)}, u32[]{:S(2)}, u32[]{:S(2)}) %all-to-all-start.1) | async-done | bytes 5242912 | tf_op jit(solution)/shard_map/all_to_all | solution.py:119
  312.7 4.7 %gather_fusion.3 = f32[32,16,1280]{2,1,0:T(8,128)} fusion(f32[64,16,1280]{2,1,0:T(8,128)} %all-to-all-done.1, s32[1024]{0:T(1024)S(1)} %pad_clamp_fusion), kind=kCustom, calls=%fused_computation.3 | custom fusion | bytes 5243008 | tf_op jit(solution)/shard_map/jit(_take)/gather | solution.py:120
  317.4 2.0 broadcast_select_fusion
  321.1 2.2 copy.21
  323.3 1.3 fusion.17
  325.4 6.2 %fusion = bf16[512,1024]{1,0:T(8,128)(2,1)} fusion(f32[32,16,1024]{2,1,0:T(8,128)S(1)} %slice-done, bf16[512,2048]{1,0:T(8,128)(2,1)} %all-gather.3.cloned.1.call-done, bf16[1024,2048]{1,0:T(8,128)(2,1)} %param.9), kind=kOutput, calls=%fused_computation.7 | convolution fusion | flops 2148532224 | bytes 9437184 | tf_op jit(solution)/shard_map/dot_general | solution.py:129
  (79 shorter events, 12.9 us)
Async XLA Ops:
  7.2 95.3 %copy-start = (bf16[8,1024,64]{1,2,0:T(8,128)(2,1)S(1)}, bf16[8,1024,64]{1,2,0:T(8,128)(2,1)}, u32[]{:S(2)}) copy-start(bf16[8,1024,64]{1,2,0:T(8,128)(2,1)} %param.10) | copy-start | bytes 3145732
  17.7 11.3 %copy-start.8 = (u32[256]{0:T(256)S(1)}, u32[256]{0:T(256)}, u32[]{:S(2)}) copy-start(u32[256]{0:T(256)} %constant.123) | copy-start | bytes 3076
  17.7 12.6 %copy-start.7 = (s32[32]{0:T(128)S(1)}, s32[32]{0:T(128)}, u32[]{:S(2)}) copy-start(s32[32]{0:T(128)} %param.12) | copy-start | bytes 388
  17.7 74.4 %copy-start.1 = (s32[256]{0:T(256)S(1)}, s32[256]{0:T(256)}, u32[]{:S(2)}) copy-start(s32[256]{0:T(256)} %param.13) | copy-start | bytes 3076
  17.7 82.9 %all-to-all-start = ((bf16[64,16,1280]{2,1,0:T(8,128)(2,1)}), bf16[64,16,1280]{2,1,0:T(8,128)(2,1)}, u32[]{:S(2)}, u32[]{:S(2)}) async-start(bf16[64,16,1280]{2,1,0:T(8,128)(2,1)} %select_select_fusion), calls=%async_computation.1 | async-start | bytes 5242880 | tf_op jit(solution)/shard_map/all_to_all | solution.py:56
  29.0 144.9 %all-reduce.3.cloned.1.call-start = ((), (), s32[]{:S(2)}) async-start(), calls=%async_computation.4 | async-start | bytes 1048576 | tf_op jit(solution)/shard_map/psum | solution.py:90
  103.7 2.2 copy-start.6
  105.1 0.8 copy-start.3
  107.3 216.0 %reduce-scatter.2.cloned.1.call-start = ((), (), s32[]{:S(2)}) async-start(), calls=%async_computation.3 | async-start | bytes 4718592 | tf_op jit(solution)/shard_map/reduce_scatter | solution.py:121
  114.3 0.7 copy-start.5
  173.9 2.5 copy-start.4
  180.6 132.1 %all-to-all-start.1 = ((f32[64,16,1280]{2,1,0:T(8,128)}), f32[64,16,1280]{2,1,0:T(8,128)}, u32[]{:S(2)}, u32[]{:S(2)}) async-start(f32[64,16,1280]{2,1,0:T(8,128)} %pad_maximum_fusion), calls=%async_computation.2 | async-start | bytes 10485760 | tf_op jit(solution)/shard_map/all_to_all | solution.py:119
  190.2 135.2 %all-gather.3.cloned.1.call-start = ((), (), s32[]{:S(2)}) async-start(), calls=%async_computation.5 | async-start | bytes 2359296 | tf_op jit(solution)/shard_map/all_gather | solution.py:130
  319.4 1.7 copy-start.2
  321.1 4.3 %slice-start = ((f32[32,16,1280]{2,1,0:T(8,128)}), f32[32,16,1024]{2,1,0:T(8,128)S(1)}, s32[]{:S(2)}) async-start(f32[32,16,1280]{2,1,0:T(8,128)} %copy-done.2), calls=%async_computation.6 | async-start | bytes 4194304 | tf_op jit(solution)/shard_map/slice | solution.py:139
Sparse Core Ops, SparseCore 0:
  107.4 66.4 all-reduce.2
  176.4 40.2 reduce-scatter.1
  218.6 29.6 all-gather.2
where the time goes:
time: 339 us; the launch traced here: 338 us
  waiting for transfers between devices  175 us (52%)
  blocking collectives  61.4 us (18%)
  local copies, waits for them, and re-layouts  26.4 us (8%)
  matrix products  22.5 us (7%)
  starting transfers between devices  21.2 us (6%)
  other arithmetic  16.6 us (5%)
  between operations  14.7 us (4%)
    all_to_all x1, waiting for transfers between devices, per_device(): lax.all_to_all(back, 'tok', split_axis=0, concat_axis=0, tiled=True)  117 us
    unnamed x1, blocking collectives  61.4 us
    psum x1, waiting for transfers between devices, per_device(): both = lax.psum(jnp.concatenate([low_part, pull_part], axis=1), 'tp')  57.9 us
    all_to_all x1, starting transfers between devices, per_device(): lax.all_to_all(send, 'tok', split_axis=0, concat_axis=0, tiled=True)  11.2 us
    all_to_all x1, starting transfers between devices, per_device(): lax.all_to_all(back, 'tok', split_axis=0, concat_axis=0, tiled=True)  9.63 us
    dot_general x1, matrix products, per_device(): lax.dot_general(frozen_weight, tokens, (((0,), (1,)), ((), ())), preferre...  6.97 us
    gather x2, local copies, waits for them, and re-layouts, per_device(): all_slot = jnp.take(slot_per_adapter, all_blocks)  6.9 us
  transfers between devices with their start and end apart: 5, of which 2 were waited for; matrix products, arithmetic and copies ran while one was open for 12% of the time, Pallas kernels for 0%

commit v1 on v0

--- a/solution.py
+++ b/solution.py
@@ -87,7 +87,7 @@
         "hs,gbs->hgb", grad_rows, adapter_up_matrices, preferred_element_type=jnp.float32
     )
     pull_part = jnp.sum(gathered_every_row * chosen_float[:, :, None], axis=1)
-    both = lax.psum(jnp.concatenate([low_part, pull_part], axis=1), "tp")
+    both = jnp.sum(lax.all_gather(jnp.concatenate([low_part, pull_part], axis=1), "tp"), axis=0)
     low_sum = both[:, :rank_ceiling]
     pull_sum = both[:, rank_ceiling:]
     reduced_rows = jnp.where(keep_cols, low_sum, 0.0).astype(jnp.bfloat16)

time: 339 us -> 312 us (0.920)
  waiting for transfers between devices: 175 us -> 142 us
  local copies, waits for them, and re-layouts: 26.4 us -> 31.9 us
    psum x1 -> x0, waiting for transfers between devices: 57.9 us -> none  [per_device(): both = lax.psum(jnp.concatenate([low_part, pull_part], axis=1), 'tp')]
    all_gather x0 -> x1, waiting for transfers between devices: none -> 26 us  [per_device(): lax.all_gather(jnp.concatenate([low_part, pull_part], axis=1), 'tp')]
    unnamed x22 -> x23, local copies, waits for them, and re-layouts: 3.89 us -> 9.33 us
  transfers between devices with their start and end apart: 5 -> 5, of which waited for: 2 -> 2; matrix products, arithmetic and copies ran while one was open for 12% -> 15% of each run, Pallas kernels for 0% -> 0%
where the time goes in v1:
time: 312 us; the launch traced here: 309 us
  waiting for transfers between devices  142 us (46%)
  blocking collectives  61.4 us (20%)
  local copies, waits for them, and re-layouts  31.9 us (10%)
  matrix products  21.5 us (7%)
  starting transfers between devices  21.4 us (7%)
  other arithmetic  16.5 us (5%)
  between operations  14.7 us (5%)
    all_to_all x1, waiting for transfers between devices, per_device(): lax.all_to_all(back, 'tok', split_axis=0, concat_axis=0, tiled=True)  115 us
    unnamed x1, blocking collectives  61.4 us
    all_gather x1, waiting for transfers between devices, per_device(): lax.all_gather(jnp.concatenate([low_part, pull_part], axis=1), 'tp')  26 us
    all_to_all x1, starting transfers between devices, per_device(): lax.all_to_all(send, 'tok', split_axis=0, concat_axis=0, tiled=True)  11.2 us
    all_to_all x1, starting transfers between devices, per_device(): lax.all_to_all(back, 'tok', split_axis=0, concat_axis=0, tiled=True)  9.63 us
    unnamed x23, local copies, waits for them, and re-layouts  9.33 us
    dot_general x1, matrix products, per_device(): lax.dot_general(frozen_weight, tokens, (((0,), (1,)), ((), ())), preferre...  6.97 us
    gather x2, local copies, waits for them, and re-layouts, per_device(): all_slot = jnp.take(slot_per_adapter, all_blocks)  6.9 us
  transfers between devices with their start and end apart: 5, of which 2 were waited for; matrix products, arithmetic and copies ran while one was open for 15% of the time, Pallas kernels for 0%

profile of v1, /device:TPU:27, one launch (start us, length us, event | category | flops | bytes accessed | tf_op | source)
XLA Modules:
  0.0 309.3 jit_solution(3348856729839203404)
XLA Ops:
  7.9 1.4 gather_fusion
  10.4 1.4 pad_maximum_fusion.1
  11.8 2.2 gather_fusion.2
  14.1 3.7 %select_select_fusion = bf16[64,16,1280]{2,1,0:T(8,128)(2,1)} fusion(bf16[64,16,1280]{2,1,0:T(8,128)(2,1)} %gather_fusion.2, pred[64]{0:T(512)(128)(4,1)S(1)} %compare_and_fusion, pred[64]{0:T(512)(128)(4,1)S(1)} %fusion.30), kind=kLoop, calls=%fused_computation.6 | loop fusion | flops 2621440 | bytes 5243008 | tf_op jit(solution)/shard_map/jit(_where)/select_n | solution.py:55
  17.7 11.2 %all-to-all-start = ((bf16[64,16,1280]{2,1,0:T(8,128)(2,1)}), bf16[64,16,1280]{2,1,0:T(8,128)(2,1)}, u32[]{:S(2)}, u32[]{:S(2)}) async-start(bf16[64,16,1280]{2,1,0:T(8,128)(2,1)} %select_select_fusion), calls=%async_computation.1 | async-start | bytes 5242880 | tf_op jit(solution)/shard_map/all_to_all | solution.py:56
  30.5 61.4 %all-reduce = s32[1024]{0:T(1024)S(1)} all-reduce(s32[1024]{0:T(1024)S(1)} %dynamic-update-slice), channel_id=2, replica_groups=mesh['tok'=32,'tp'=8] {'tok'}, use_global_device_ids=true, to_apply=%add | all-reduce | flops 1024 | bytes 8192
  92.1 6.8 %gather_fusion.1 = s32[1024]{0:T(1024)S(1)} fusion(s32[256]{0:T(256)S(1)} %copy-done.1, s32[1024]{0:T(1024)S(1)} %broadcast_clamp_fusion), kind=kCustom, calls=%fused_computation.1 | custom fusion | bytes 12288 | tf_op jit(solution)/shard_map/jit(_take)/gather | solution.py:58
  100.6 1.8 slice.32
  102.5 1.3 fusion.37
  104.0 1.1 slice.33
  107.5 7.0 %fusion.36 = f32[2048,512]{1,0:T(8,128)} fusion(bf16[1024,2048]{1,0:T(8,128)(2,1)} %param.9, bf16[512,1024]{1,0:T(8,128)(2,1)} %param.8), kind=kOutput, calls=%fused_computation.87 | convolution fusion | flops 2147483648 | bytes 9437184 | tf_op jit(solution)/shard_map/dot_general | solution.py:122
  116.2 26.0 %all-gather.7.cloned.1.call-done = f32[8192,128]{0,1:T(8,128)} async-done(((f32[1024,128]{0,1:T(8,128)}), f32[8192,128]{0,1:T(8,128)}) %all-gather.7.cloned.1.call-update) | async-done | bytes 4194320 | tf_op jit(solution)/shard_map/all_gather | solution.py:90
  142.1 5.4 %copy.26 = f32[16,8,8,1024]{3,2,1,0:T(8,128)S(1)} copy(f32[16,8,8,1024]{3,1,2,0:T(8,128)} %bitcast.58) | data formatting | bytes 8388608
  149.2 1.3 fusion.6
  150.5 2.9 pad_maximum_fusion
  153.3 9.6 %all-to-all-start.1 = ((f32[64,16,1280]{2,1,0:T(8,128)}), f32[64,16,1280]{2,1,0:T(8,128)}, u32[]{:S(2)}, u32[]{:S(2)}) async-start(f32[64,16,1280]{2,1,0:T(8,128)} %pad_maximum_fusion), calls=%async_computation.2 | async-start | bytes 10485760 | tf_op jit(solution)/shard_map/all_to_all | solution.py:119
  163.7 2.3 fusion.14
  166.0 2.6 convolution_bitcast_fusion
  168.6 115.4 %all-to-all-done.1 = f32[64,16,1280]{2,1,0:T(8,128)} async-done(((f32[64,16,1280]{2,1,0:T(8,128)}), f32[64,16,1280]{2,1,0:T(8,128)}, u32[]{:S(2)}, u32[]{:S(2)}) %all-to-all-start.1) | async-done | bytes 5242912 | tf_op jit(solution)/shard_map/all_to_all | solution.py:119
  283.9 4.7 %gather_fusion.3 = f32[32,16,1280]{2,1,0:T(8,128)} fusion(f32[64,16,1280]{2,1,0:T(8,128)} %all-to-all-done.1, s32[1024]{0:T(1024)S(1)} %pad_clamp_fusion), kind=kCustom, calls=%fused_computation.3 | custom fusion | bytes 5243008 | tf_op jit(solution)/shard_map/jit(_take)/gather | solution.py:120
  288.7 2.0 broadcast_select_fusion
  292.3 2.2 copy.24
  294.5 1.3 fusion.17
  296.6 6.2 %fusion = bf16[512,1024]{1,0:T(8,128)(2,1)} fusion(f32[32,16,1024]{2,1,0:T(8,128)S(1)} %slice-done, bf16[512,2048]{1,0:T(8,128)(2,1)} %all-gather.5.cloned.1.call-done, bf16[1024,2048]{1,0:T(8,128)(2,1)} %param.9), kind=kOutput, calls=%fused_computation.8 | convolution fusion | flops 2148532224 | bytes 9437184 | tf_op jit(solution)/shard_map/dot_general | solution.py:129
  (81 shorter events, 13.5 us)
Async XLA Ops:
  7.2 95.3 %copy-start = (bf16[8,1024,64]{1,2,0:T(8,128)(2,1)S(1)}, bf16[8,1024,64]{1,2,0:T(8,128)(2,1)}, u32[]{:S(2)}) copy-start(bf16[8,1024,64]{1,2,0:T(8,128)(2,1)} %param.10) | copy-start | bytes 3145732
  17.7 11.3 %copy-start.8 = (u32[256]{0:T(256)S(1)}, u32[256]{0:T(256)}, u32[]{:S(2)}) copy-start(u32[256]{0:T(256)} %constant.123) | copy-start | bytes 3076
  17.7 12.6 %copy-start.7 = (s32[32]{0:T(128)S(1)}, s32[32]{0:T(128)}, u32[]{:S(2)}) copy-start(s32[32]{0:T(128)} %param.12) | copy-start | bytes 388
  17.7 74.4 %copy-start.1 = (s32[256]{0:T(256)S(1)}, s32[256]{0:T(256)}, u32[]{:S(2)}) copy-start(s32[256]{0:T(256)} %param.13) | copy-start | bytes 3076
  17.7 82.9 %all-to-all-start = ((bf16[64,16,1280]{2,1,0:T(8,128)(2,1)}), bf16[64,16,1280]{2,1,0:T(8,128)(2,1)}, u32[]{:S(2)}, u32[]{:S(2)}) async-start(bf16[64,16,1280]{2,1,0:T(8,128)(2,1)} %select_select_fusion), calls=%async_computation.1 | async-start | bytes 5242880 | tf_op jit(solution)/shard_map/all_to_all | solution.py:56
  29.0 113.1 %all-gather.7.cloned.1.call-start = ((), (), s32[]{:S(2)}) async-start(), calls=%async_computation.5 | async-start | bytes 4718592 | tf_op jit(solution)/shard_map/all_gather | solution.py:90
  103.7 2.2 copy-start.5
  105.1 0.8 copy-start.3
  107.3 187.2 %reduce-scatter.2.cloned.1.call-start = ((), (), s32[]{:S(2)}) async-start(), calls=%async_computation.3 | async-start | bytes 4718592 | tf_op jit(solution)/shard_map/reduce_scatter | solution.py:121
  114.5 0.7 copy-start.4
  147.5 1.1 copy-start.6
  153.3 130.6 %all-to-all-start.1 = ((f32[64,16,1280]{2,1,0:T(8,128)}), f32[64,16,1280]{2,1,0:T(8,128)}, u32[]{:S(2)}, u32[]{:S(2)}) async-start(f32[64,16,1280]{2,1,0:T(8,128)} %pad_maximum_fusion), calls=%async_computation.2 | async-start | bytes 10485760 | tf_op jit(solution)/shard_map/all_to_all | solution.py:119
  162.9 133.7 %all-gather.5.cloned.1.call-start = ((), (), s32[]{:S(2)}) async-start(), calls=%async_computation.4 | async-start | bytes 2359296 | tf_op jit(solution)/shard_map/all_gather | solution.py:130
  290.6 1.7 copy-start.2
  292.3 4.3 %slice-start = ((f32[32,16,1280]{2,1,0:T(8,128)}), f32[32,16,1024]{2,1,0:T(8,128)S(1)}, s32[]{:S(2)}) async-start(f32[32,16,1280]{2,1,0:T(8,128)} %copy-done.2), calls=%async_computation.6 | async-start | bytes 4194304 | tf_op jit(solution)/shard_map/slice | solution.py:139
Sparse Core Ops, SparseCore 0:
  107.4 34.6 all-gather.6
  144.7 41.0 reduce-scatter.1
  187.6 29.7 all-gather.4
